TPU v7x, 256 devices: a whole 4x4x8 slice. The times are simulated.
256 devices in a mesh: row: 32 (over z, y), col: 8 (over x, core).
Axes of the slice: x: 4, y: 4, z: 8, core: 2. Of those that a mesh axis runs over, the one named last changes fastest.
Arguments:
- amps: bfloat16 [30720, 30720], P(('col', 'row')), may hold values from -6 to 6
- cycle_int: bfloat16 [30720, 1024], P('col'), may hold values from -0.03125 to 0.03125
- tile_mask: int32 [480, 16], P('col'), may hold values 0 or 1
- coulomb: bfloat16 [30720, 1024], P('row', 'col'), may hold values from -6 to 6
- occ_irrep: int32 [240], replicated, may hold values from 0 to 7
- vir_irrep: int32 [192], replicated, may hold values from 0 to 7
- occ_energy: float32 [240], replicated, may hold values from -1.5 to -0.3
- vir_energy: float32 [192], replicated, may hold values from 0.3 to 2
Outputs:
- new_amps: bfloat16 [30720, 1024], P('row', 'col')
All inputs are finite; a program needn't handle non-finite values. No bound on the sum of `tile_mask` on one device may be relied on, other than what follows from the above.
Results may differ from a plain program's by a relative error of at most 0.001.
Values may be sent and summed in bfloat16 or wider, within the bound.
No kernel may reach another device: no remote copies, remote signals or barrier semaphores. Data moves between devices by JAX's collectives and lax.ppermute only.
A program may use at most 128 MiB of HBM per device.

v0:
```python
import jax
import jax.numpy as jnp
from jax import lax
from jax.sharding import Mesh, PartitionSpec as P

BLK = 64
Z, Y, X, C = ("z", "y", "x", "core")
COL = (X, C)
ROW = (Z, Y)


def lookup(positions, values_table):
    entries = jnp.arange(values_table.shape[0], dtype=jnp.int32)
    picked = jnp.where(
        positions[:, None] == entries[None, :],
        values_table[None, :],
        jnp.zeros((), values_table.dtype),
    )
    return jnp.sum(picked, axis=1)


def swap_perm(nz, nc):
    return [(z * nc + c, c * nz + z) for z in range(nz) for c in range(nc)]


def local(amps, cycle_int, tile_mask, coulomb, occ_irrep, vir_irrep, occ_energy, vir_energy):
    block_size = BLK
    occupied = occ_energy.shape[0]
    row_blocks = vir_energy.shape[0] // block_size - 1
    kc_rows, jb_all = cycle_int.shape
    rows_here, cols_here = coulomb.shape
    nz = lax.axis_size(Z)
    ny = lax.axis_size(Y)
    ncol = lax.axis_size(COL)
    z = lax.axis_index(Z)
    y = lax.axis_index(Y)
    c = lax.axis_index(COL)
    sub = amps.shape[0]
    span = sub * ny
    ci_rows = lax.dynamic_slice_in_dim(cycle_int, z * span, span, axis=0)
    mask_rows = jnp.repeat(tile_mask.astype(jnp.bfloat16), block_size, axis=0)
    mask_rows = lax.dynamic_slice_in_dim(mask_rows, z * span, span, axis=0)
    masked = (
        ci_rows.reshape(span, jb_all // block_size, block_size) * mask_rows[:, :, None]
    ).reshape(span, jb_all)
    masked_all = lax.all_gather(masked, COL, axis=0, tiled=True)
    plane_amps = lax.all_to_all(amps, (X, C, Y), split_axis=1, concat_axis=0, tiled=True)
    partial_value = lax.dot_general(
        plane_amps, masked_all, (((0,), (0,)), ((), ())), preferred_element_type=jnp.float32
    )
    cycle_sum = lax.psum_scatter(partial_value, Z, scatter_dimension=1, tiled=True)
    perm = swap_perm(nz, ncol)
    coulomb_here = lax.ppermute(coulomb, (Z, X, C), perm)
    row_block = c * ny + y
    row_pos = row_block * rows_here + jnp.arange(rows_here, dtype=jnp.int32)
    col_pos = z * cols_here + jnp.arange(cols_here, dtype=jnp.int32)
    occ_row = row_pos // block_size % occupied
    vir_row = block_size * (row_pos // (occupied * block_size)) + row_pos % block_size
    occ_col = col_pos // block_size % occupied
    vir_col = col_pos % block_size + row_blocks * block_size
    sym_row = jnp.bitwise_xor(lookup(occ_row, occ_irrep), lookup(vir_row, vir_irrep))
    sym_col = jnp.bitwise_xor(lookup(occ_col, occ_irrep), lookup(vir_col, vir_irrep))
    allowed = sym_row[:, None] == sym_col[None, :]
    gap_row = lookup(vir_row, vir_energy) - lookup(occ_row, occ_energy)
    gap_col = lookup(vir_col, vir_energy) - lookup(occ_col, occ_energy)
    denominator = gap_row[:, None] + gap_col[None, :]
    updated = (coulomb_here.astype(jnp.float32) + cycle_sum) / denominator
    out = jnp.where(allowed, updated, jnp.float32(0.0)).astype(jnp.bfloat16)
    return lax.ppermute(out, (Z, X, C), perm)


def solution(mesh):
    nrow, ncol = mesh.devices.shape
    ncore = 2
    nx = ncol // ncore
    nz = ncol
    ny = nrow // nz
    torus = Mesh(mesh.devices.reshape(nz, ny, nx, ncore), (Z, Y, X, C))
    return jax.shard_map(
        local,
        mesh=torus,
        in_specs=(P(COL + ROW, None), P(COL, None), P(COL, None), P(ROW, COL), P(), P(), P(), P()),
        out_specs=P(ROW, COL),
        check_vma=False,
    )
```

profile of v0, /device:TPU:7, one launch (start us, length us, event | category | flops | bytes accessed | tf_op | source)
XLA Modules:
  0.0 276.8 jit_solution(13097134514686713037)
XLA Ops:
  6.5 1.3 constant_dynamic-slice_fusion
  7.8 0.5 copy.22
  8.4 0.7 convert_element_type.10
  9.1 0.2 broadcast_in_dim.140
  9.3 0.3 reshape.119
  9.5 0.1 constant_dynamic-slice_fusion.1
  9.6 0.1 bitcast_multiply_fusion
  9.7 1.4 copy.19
  11.1 0.0 all-gather.2.cloned.1.call-update
  11.1 0.0 reduce-scatter.2.cloned.1.call-start
  11.1 10.1 %copy.20 = bf16[120,30720]{0,1:T(8,128)(2,1)} copy(bf16[120,30720]{1,0:T(8,128)(2,1)} %param.8) | data formatting | bytes 14745600 | tf_op args[0]
  21.3 126.3 %all_to_all.19 = bf16[120,32,960]{0,2,1:T(8,128)(2,1)S(1)} all-to-all(bf16[120,32,960]{0,2,1:T(8,128)(2,1)} %bitcast.13), channel_id=1, replica_groups=mesh['z'=8,'y'=4,'x'=4,'core'=2] {'x','core','y'}, dimensions={1} | all-to-all | bytes 14745600 | tf_op jit(solution)/shard_map/all_to_all | solution.py:47
  147.6 8.2 %copy.21 = bf16[32,120,960]{1,0,2:T(8,128)(2,1)} copy(bf16[32,120,960]{1,2,0:T(8,128)(2,1)S(1)} %bitcast.12) | data formatting | bytes 14745600 | tf_op jit(solution)/shard_map/all_to_all | solution.py:47
  155.8 15.6 %all_to_all.17 = bf16[3840,960]{0,1:T(8,128)(2,1)} reshape(bf16[32,120,960]{1,0,2:T(8,128)(2,1)} %copy.21) | data formatting | bytes 14745600 | tf_op jit(solution)/shard_map/all_to_all | solution.py:47
  171.5 0.0 all-gather.2.cloned.1.call-done
  171.5 13.7 %convolution_bitcast_fusion = f32[960,1024]{1,0:T(8,128)} fusion(bf16[3840,960]{0,1:T(8,128)(2,1)} %all_to_all.17, bf16[3840,1024]{1,0:T(8,128)(2,1)} %all-gather.2.cloned.1.call-done), kind=kOutput, calls=%fused_computation | convolution fusion | flops 7549747200 | bytes 19169280 | tf_op jit(solution)/shard_map/dot_general | solution.py:48
  185.2 0.0 reduce-scatter.2.cloned.1.call-update
  185.2 6.9 %collective-permute-start = (bf16[960,128]{1,0:T(8,128)(2,1)S(1)}, bf16[960,128]{1,0:T(8,128)(2,1)S(1)}, u32[]{:S(2)}, u32[]{:S(2)}) collective-permute-start(bf16[960,128]{1,0:T(8,128)(2,1)S(1)} %copy-done.4), channel_id=1, source_target_pairs={{0,0},{1,32},{2,64},{3,96},{4,128},{5,160},{6,192},{7,224},{32,1},... | collective-permute-start | bytes 737288 | tf_op jit(solution)/shard_map/ppermute | solution.py:53
  192.1 0.1 select_reduce_fusion.6
  192.2 0.1 select_reduce_fusion.4
  192.4 0.2 select_reduce_fusion.2
  192.6 0.4 select_reduce_fusion
  193.0 0.1 select_reduce_fusion.7
  193.1 0.1 select_reduce_fusion.5
  193.2 0.2 select_reduce_fusion.3
  193.4 0.4 select_reduce_fusion.1
  193.8 19.5 %collective-permute-done = bf16[960,128]{1,0:T(8,128)(2,1)S(1)} collective-permute-done((bf16[960,128]{1,0:T(8,128)(2,1)S(1)}, bf16[960,128]{1,0:T(8,128)(2,1)S(1)}, u32[]{:S(2)}, u32[]{:S(2)}) %collective-permute-start) | collective-permute-done | bytes 245792 | tf_op jit(solution)/shard_map/ppermute | solution.py:53
  213.3 33.6 %reduce-scatter.2.cloned.1.call-done = f32[960,128]{1,0:T(8,128)} async-done(((f32[960,1024]{1,0:T(8,128)}), f32[960,128]{1,0:T(8,128)}) %reduce-scatter.2.cloned.1.call-update) | async-done | bytes 491536 | tf_op jit(solution)/shard_map/reduce_scatter | solution.py:51
  246.8 1.3 select_convert_fusion
  248.2 3.0 %collective-permute-start.1 = (bf16[960,128]{1,0:T(8,128)(2,1)S(1)}, bf16[960,128]{1,0:T(8,128)(2,1)S(1)}, u32[]{:S(2)}, u32[]{:S(2)}) collective-permute-start(bf16[960,128]{1,0:T(8,128)(2,1)S(1)} %select_convert_fusion), channel_id=1, source_target_pairs={{0,0},{1,32},{2,64},{3,96},{4,128},{5,160},{6,192},{7,224},{32,1},... | collective-permute-start | bytes 737288 | tf_op jit(solution)/shard_map/ppermute | solution.py:69
  251.2 18.0 %collective-permute-done.1 = bf16[960,128]{1,0:T(8,128)(2,1)S(1)} collective-permute-done((bf16[960,128]{1,0:T(8,128)(2,1)S(1)}, bf16[960,128]{1,0:T(8,128)(2,1)S(1)}, u32[]{:S(2)}, u32[]{:S(2)}) %collective-permute-start.1) | collective-permute-done | bytes 245792 | tf_op jit(solution)/shard_map/ppermute | solution.py:69
  269.3 0.7 copy.24
  (17 shorter events, 0.1 us)
Async XLA Ops:
  6.5 164.9 %all-gather.2.cloned.1.call-start = ((), (), s32[]{:S(2)}) async-start(), calls=%async_computation.2 | async-start | bytes 8847360 | tf_op jit(solution)/shard_map/all_gather | solution.py:46
  11.1 235.7 %reduce-scatter.2.cloned.1.call-start = ((), (), s32[]{:S(2)}) async-start(), calls=%async_computation.3 | async-start | bytes 4423680 | tf_op jit(solution)/shard_map/reduce_scatter | solution.py:51
  171.4 13.8 %copy-start.4 = (bf16[960,128]{1,0:T(8,128)(2,1)S(1)}, bf16[960,128]{1,0:T(8,128)(2,1)}, u32[]{:S(2)}) copy-start(bf16[960,128]{1,0:T(8,128)(2,1)} %param.11) | copy-start | bytes 737284
  171.4 20.7 %copy-start = (f32[192]{0:T(256)S(1)}, f32[192]{0:T(256)}, u32[]{:S(2)}) copy-start(f32[192]{0:T(256)} %param.15) | copy-start | bytes 2308
  171.4 20.8 %copy-start.1 = (f32[240]{0:T(256)S(1)}, f32[240]{0:T(256)}, u32[]{:S(2)}) copy-start(f32[240]{0:T(256)} %param.14) | copy-start | bytes 2884
  171.4 21.5 %copy-start.2 = (s32[192]{0:T(256)S(1)}, s32[192]{0:T(256)}, u32[]{:S(2)}) copy-start(s32[192]{0:T(256)} %param.13) | copy-start | bytes 2308
  171.4 21.6 %copy-start.3 = (s32[240]{0:T(256)S(1)}, s32[240]{0:T(256)}, u32[]{:S(2)}) copy-start(s32[240]{0:T(256)} %param.12) | copy-start | bytes 2884
  185.2 28.1 %collective-permute-start = (bf16[960,128]{1,0:T(8,128)(2,1)S(1)}, bf16[960,128]{1,0:T(8,128)(2,1)S(1)}, u32[]{:S(2)}, u32[]{:S(2)}) collective-permute-start(bf16[960,128]{1,0:T(8,128)(2,1)S(1)} %copy-done.4), channel_id=1, source_target_pairs={{0,0},{1,32},{2,64},{3,96},{4,128},{5,160},{6,192},{7,224},{32,1},... | collective-permute-start | bytes 737288 | tf_op jit(solution)/shard_map/ppermute | solution.py:53
  248.2 21.1 %collective-permute-start.1 = (bf16[960,128]{1,0:T(8,128)(2,1)S(1)}, bf16[960,128]{1,0:T(8,128)(2,1)S(1)}, u32[]{:S(2)}, u32[]{:S(2)}) collective-permute-start(bf16[960,128]{1,0:T(8,128)(2,1)S(1)} %select_convert_fusion), channel_id=1, source_target_pairs={{0,0},{1,32},{2,64},{3,96},{4,128},{5,160},{6,192},{7,224},{32,1},... | collective-permute-start | bytes 737288 | tf_op jit(solution)/shard_map/ppermute | solution.py:69
Sparse Core Ops, SparseCore 0:
  11.2 113.2 all-gather.1
  185.3 61.4 reduce-scatter.1
where the time goes:
time: 278 us; the launch traced here: 277 us
  blocking collectives  126 us (45%)
  waiting for transfers between devices  71.2 us (26%)
  local copies, waits for them, and re-layouts  38.4 us (14%)
  matrix products  13.7 us (5%)
  between operations  13.6 us (5%)
  starting transfers between devices  9.94 us (4%)
  other arithmetic  3.68 us (1%)
    all_to_all x1, blocking collectives, local(): lax.all_to_all(amps, (X, C, Y), split_axis=1, concat_axis=0, tiled=True)  126 us
    reduce_scatter x1, waiting for transfers between devices, local(): lax.psum_scatter(partial_value, Z, scatter_dimension=1, tiled=True)  33.6 us
    all_to_all x2, local copies, waits for them, and re-layouts, local(): lax.all_to_all(amps, (X, C, Y), split_axis=1, concat_axis=0, tiled=True)  23.9 us
    ppermute x1, waiting for transfers between devices, local(): coulomb_here = lax.ppermute(coulomb, (Z, X, C), perm)  19.5 us
    ppermute x1, waiting for transfers between devices, local(): return lax.ppermute(out, (Z, X, C), perm)  18 us
    dot_general x1, matrix products, local(): lax.dot_general(plane_amps, masked_all, (((0,), (0,)), ((), ())), preferr...  13.7 us
    unnamed x13, local copies, waits for them, and re-layouts  11.4 us
    ppermute x1, starting transfers between devices, local(): coulomb_here = lax.ppermute(coulomb, (Z, X, C), perm)  6.88 us
  transfers between devices with their start and end apart: 4, of which 3 were waited for; matrix products, arithmetic and copies ran while one was open for 7% of the time, Pallas kernels for 0%

commit v1 on v0

--- a/solution.py
+++ b/solution.py
@@ -44,7 +44,12 @@
         ci_rows.reshape(span, jb_all // block_size, block_size) * mask_rows[:, :, None]
     ).reshape(span, jb_all)
     masked_all = lax.all_gather(masked, COL, axis=0, tiled=True)
-    plane_amps = lax.all_to_all(amps, (X, C, Y), split_axis=1, concat_axis=0, tiled=True)
+    plane_amps = jnp.concatenate(
+        lax.all_to_all(
+            jnp.stack(jnp.split(amps, lax.axis_size((X, C, Y)), axis=1)), (X, C, Y), 0, 0
+        ),
+        axis=0,
+    )
     partial_value = lax.dot_general(
         plane_amps, masked_all, (((0,), (0,)), ((), ())), preferred_element_type=jnp.float32
     )

time: 278 us -> 255 us (0.917)
  blocking collectives: 126 us -> 103 us
    all_to_all x2 -> x0, local copies, waits for them, and re-layouts: 23.9 us -> none  [local(): lax.all_to_all(amps, (X, C, Y), split_axis=1, concat_axis=0, tiled=True)]
    all_to_all x1, blocking collectives: 126 us -> 103 us  [local(): lax.all_to_all(jnp.stack(jnp.split(amps, lax.axis_size((X, C, Y)), axis=1...]
    unnamed x13 -> x43, local copies, waits for them, and re-layouts: 11.4 us -> 33.2 us
  transfers between devices with their start and end apart: 4 -> 4, of which waited for: 3 -> 3; matrix products, arithmetic and copies ran while one was open for 7% -> 14% of each run, Pallas kernels for 0% -> 0%
where the time goes in v1:
time: 255 us; the launch traced here: 253 us
  blocking collectives  103 us (40%)
  waiting for transfers between devices  71.3 us (28%)
  local copies, waits for them, and re-layouts  37.4 us (15%)
  matrix products  13.8 us (5%)
  between operations  13.8 us (5%)
  starting transfers between devices  10.2 us (4%)
  other arithmetic  3.68 us (1%)
    all_to_all x1, blocking collectives, local(): lax.all_to_all(jnp.stack(jnp.split(amps, lax.axis_size((X, C, Y)), axis=1...  103 us
    reduce_scatter x1, waiting for transfers between devices, local(): lax.psum_scatter(partial_value, Z, scatter_dimension=1, tiled=True)  33.4 us
    unnamed x43, local copies, waits for them, and re-layouts  33.2 us
    ppermute x1, waiting for transfers between devices, local(): coulomb_here = lax.ppermute(coulomb, (Z, X, C), perm)  19.5 us
    ppermute x1, waiting for transfers between devices, local(): return lax.ppermute(out, (Z, X, C), perm)  18.3 us
    dot_general x1, matrix products, local(): lax.dot_general(plane_amps, masked_all, (((0,), (0,)), ((), ())), preferr...  13.8 us
    ppermute x1, starting transfers between devices, local(): coulomb_here = lax.ppermute(coulomb, (Z, X, C), perm)  7.07 us
  transfers between devices with their start and end apart: 4, of which 3 were waited for; matrix products, arithmetic and copies ran while one was open for 14% of the time, Pallas kernels for 0%

profile of v1, /device:TPU:7, one launch (start us, length us, event | category | flops | bytes accessed | tf_op | source)
XLA Modules:
  0.0 253.4 jit_solution(12719601767798529318)
XLA Ops:
  6.5 1.3 constant_dynamic-slice_fusion
  9.7 1.3 copy.15
  12.1 1.1 bitcast_dynamic-update-slice_fusion.30
  13.2 1.0 bitcast_dynamic-update-slice_fusion.29
  14.1 1.1 bitcast_dynamic-update-slice_fusion.28
  16.2 1.1 bitcast_dynamic-update-slice_fusion.26
  18.2 1.1 bitcast_dynamic-update-slice_fusion.24
  20.3 1.1 bitcast_dynamic-update-slice_fusion.22
  22.4 1.1 bitcast_dynamic-update-slice_fusion.20
  24.4 1.1 bitcast_dynamic-update-slice_fusion.18
  25.5 1.0 bitcast_dynamic-update-slice_fusion.17
  26.5 1.1 bitcast_dynamic-update-slice_fusion.16
  27.7 1.0 bitcast_dynamic-update-slice_fusion.15
  28.7 1.1 bitcast_dynamic-update-slice_fusion.14
  30.7 1.1 bitcast_dynamic-update-slice_fusion.12
  31.8 1.0 bitcast_dynamic-update-slice_fusion.11
  32.8 1.1 bitcast_dynamic-update-slice_fusion.10
  34.9 1.1 bitcast_dynamic-update-slice_fusion.8
  37.0 1.1 bitcast_dynamic-update-slice_fusion.6
  38.1 1.0 bitcast_dynamic-update-slice_fusion.5
  39.1 1.1 bitcast_dynamic-update-slice_fusion.4
  40.2 1.0 bitcast_dynamic-update-slice_fusion.3
  41.1 1.1 bitcast_dynamic-update-slice_fusion.2
  43.2 1.1 bitcast_dynamic-update-slice_fusion
  44.3 103.3 %all_to_all.5 = bf16[32,120,960]{2,1,0:T(8,128)(2,1)} all-to-all(bf16[32,120,960]{2,1,0:T(8,128)(2,1)S(1)} %bitcast_dynamic-update-slice_fusion), channel_id=1, replica_groups=mesh['z'=8,'y'=4,'x'=4,'core'=2] {'x','core','y'}, dimensions={0} | all-to-all | bytes 14745600 | tf_op jit(solution)/shard_map/all_to_all | solution.py:48
  147.6 13.8 %fusion.9 = f32[960,1024]{1,0:T(8,128)} fusion(bf16[3840,960]{1,0:T(8,128)(2,1)} %bitcast.71, bf16[3840,1024]{1,0:T(8,128)(2,1)} %all-gather.2.cloned.1.call-done), kind=kOutput, calls=%fused_computation.74 | convolution fusion | flops 7549747200 | bytes 19169280 | tf_op jit(solution)/shard_map/dot_general | solution.py:53
  161.5 7.1 %collective-permute-start = (bf16[960,128]{1,0:T(8,128)(2,1)S(1)}, bf16[960,128]{1,0:T(8,128)(2,1)S(1)}, u32[]{:S(2)}, u32[]{:S(2)}) collective-permute-start(bf16[960,128]{1,0:T(8,128)(2,1)S(1)} %copy-done.4), channel_id=1, source_target_pairs={{0,0},{1,32},{2,64},{3,96},{4,128},{5,160},{6,192},{7,224},{32,1},... | collective-permute-start | bytes 737288 | tf_op jit(solution)/shard_map/ppermute | solution.py:58
  170.2 19.5 %collective-permute-done = bf16[960,128]{1,0:T(8,128)(2,1)S(1)} collective-permute-done((bf16[960,128]{1,0:T(8,128)(2,1)S(1)}, bf16[960,128]{1,0:T(8,128)(2,1)S(1)}, u32[]{:S(2)}, u32[]{:S(2)}) %collective-permute-start) | collective-permute-done | bytes 245792 | tf_op jit(solution)/shard_map/ppermute | solution.py:58
  189.7 33.4 %reduce-scatter.2.cloned.1.call-done = f32[960,128]{1,0:T(8,128)} async-done(((f32[960,1024]{1,0:T(8,128)}), f32[960,128]{1,0:T(8,128)}) %reduce-scatter.2.cloned.1.call-update) | async-done | bytes 491536 | tf_op jit(solution)/shard_map/reduce_scatter | solution.py:56
  223.2 1.3 select_convert_fusion
  224.5 3.0 %collective-permute-start.1 = (bf16[960,128]{1,0:T(8,128)(2,1)S(1)}, bf16[960,128]{1,0:T(8,128)(2,1)S(1)}, u32[]{:S(2)}, u32[]{:S(2)}) collective-permute-start(bf16[960,128]{1,0:T(8,128)(2,1)S(1)} %select_convert_fusion), channel_id=1, source_target_pairs={{0,0},{1,32},{2,64},{3,96},{4,128},{5,160},{6,192},{7,224},{32,1},... | collective-permute-start | bytes 737288 | tf_op jit(solution)/shard_map/ppermute | solution.py:74
  227.6 18.3 %collective-permute-done.1 = bf16[960,128]{1,0:T(8,128)(2,1)S(1)} collective-permute-done((bf16[960,128]{1,0:T(8,128)(2,1)S(1)}, bf16[960,128]{1,0:T(8,128)(2,1)S(1)}, u32[]{:S(2)}, u32[]{:S(2)}) %collective-permute-start.1) | collective-permute-done | bytes 245792 | tf_op jit(solution)/shard_map/ppermute | solution.py:74
  (46 shorter events, 13.9 us)
Async XLA Ops:
  6.5 141.1 %all-gather.2.cloned.1.call-start = ((), (), s32[]{:S(2)}) async-start(), calls=%async_computation.2 | async-start | bytes 8847360 | tf_op jit(solution)/shard_map/all_gather | solution.py:46
  11.0 212.1 %reduce-scatter.2.cloned.1.call-start = ((), (), s32[]{:S(2)}) async-start(), calls=%async_computation.3 | async-start | bytes 4423680 | tf_op jit(solution)/shard_map/reduce_scatter | solution.py:56
  147.6 13.8 %copy-start.4 = (bf16[960,128]{1,0:T(8,128)(2,1)S(1)}, bf16[960,128]{1,0:T(8,128)(2,1)}, u32[]{:S(2)}) copy-start(bf16[960,128]{1,0:T(8,128)(2,1)} %param.11) | copy-start | bytes 737284
  147.6 21.0 %copy-start = (f32[192]{0:T(256)S(1)}, f32[192]{0:T(256)}, u32[]{:S(2)}) copy-start(f32[192]{0:T(256)} %param.15) | copy-start | bytes 2308
  147.6 21.1 %copy-start.1 = (f32[240]{0:T(256)S(1)}, f32[240]{0:T(256)}, u32[]{:S(2)}) copy-start(f32[240]{0:T(256)} %param.14) | copy-start | bytes 2884
  147.6 21.8 %copy-start.2 = (s32[192]{0:T(256)S(1)}, s32[192]{0:T(256)}, u32[]{:S(2)}) copy-start(s32[192]{0:T(256)} %param.13) | copy-start | bytes 2308
  147.6 21.9 %copy-start.3 = (s32[240]{0:T(256)S(1)}, s32[240]{0:T(256)}, u32[]{:S(2)}) copy-start(s32[240]{0:T(256)} %param.12) | copy-start | bytes 2884
  161.5 28.3 %collective-permute-start = (bf16[960,128]{1,0:T(8,128)(2,1)S(1)}, bf16[960,128]{1,0:T(8,128)(2,1)S(1)}, u32[]{:S(2)}, u32[]{:S(2)}) collective-permute-start(bf16[960,128]{1,0:T(8,128)(2,1)S(1)} %copy-done.4), channel_id=1, source_target_pairs={{0,0},{1,32},{2,64},{3,96},{4,128},{5,160},{6,192},{7,224},{32,1},... | collective-permute-start | bytes 737288 | tf_op jit(solution)/shard_map/ppermute | solution.py:58
  224.5 21.4 %collective-permute-start.1 = (bf16[960,128]{1,0:T(8,128)(2,1)S(1)}, bf16[960,128]{1,0:T(8,128)(2,1)S(1)}, u32[]{:S(2)}, u32[]{:S(2)}) collective-permute-start(bf16[960,128]{1,0:T(8,128)(2,1)S(1)} %select_convert_fusion), channel_id=1, source_target_pairs={{0,0},{1,32},{2,64},{3,96},{4,128},{5,160},{6,192},{7,224},{32,1},... | collective-permute-start | bytes 737288 | tf_op jit(solution)/shard_map/ppermute | solution.py:74
Sparse Core Ops, SparseCore 0:
  11.2 66.0 all-gather.1
  161.6 61.5 reduce-scatter.1
